TPU v7x, 32 devices: a whole 2x2x4 slice. The times are simulated.
32 devices in a mesh: dp: 8 (over y, x, core), tensor: 4 (over z).
Axes of the slice: x: 2, y: 2, z: 4, core: 2. Of those that a mesh axis runs over, the one named last changes fastest.
Arguments:
- hidden_in: bfloat16 [16, 1024, 2048], P('dp', 'tensor'), may hold values from -6 to 6
- keep_slot: int32 [16], P('dp'), may hold values 0 or 1
- out_grad: bfloat16 [16, 1024, 2048], P('dp', 'tensor'), may hold values from -8 to 8
- ln1_gain: bfloat16 [2048], replicated, may hold values from 0.5 to 1.5
- ln1_bias: bfloat16 [2048], replicated, may hold values from -1.25 to 1.25
- ln2_gain: bfloat16 [2048], replicated, may hold values from 0.5 to 1.5
- ln2_bias: bfloat16 [2048], replicated, may hold values from -1.25 to 1.25
- qkv_weight: bfloat16 [2048, 6144], P(None, 'tensor'), may hold values from -0.125 to 0.125
- qkv_bias: bfloat16 [8, 768], P('tensor'), may hold values from -0.625 to 0.625
- dense_weight: bfloat16 [2048, 2048], P('tensor'), may hold values from -0.75 to 0.75
- dense_bias: bfloat16 [2048], replicated, may hold values from -1.25 to 1.25
- fc1_weight: bfloat16 [2048, 8192], P(None, 'tensor'), may hold values from -0.125 to 0.125
- fc1_bias: bfloat16 [8192], P('tensor'), may hold values from -1.25 to 1.25
- fc2_weight: bfloat16 [8192, 2048], P('tensor'), may hold values from -0.0625 to 0.0625
- fc2_bias: bfloat16 [2048], replicated, may hold values from -1.25 to 1.25
Outputs:
- block_out: bfloat16 [16, 1024, 2048], P('dp', 'tensor')
- hidden_grad: float32 [16, 1024, 2048], P('dp', 'tensor')
- ln1_gain_grad: float32 [2048], P(('dp', 'tensor'))
- ln1_bias_grad: float32 [2048], P(('dp', 'tensor'))
- ln2_gain_grad: float32 [2048], P(('dp', 'tensor'))
- ln2_bias_grad: float32 [2048], P(('dp', 'tensor'))
- qkv_weight_grad: float32 [2048, 6144], P('dp', 'tensor')
- qkv_bias_grad: float32 [8, 768], P('tensor', 'dp')
- dense_weight_grad: float32 [2048, 2048], P('tensor', 'dp')
- dense_bias_grad: float32 [2048], P(('dp', 'tensor'))
- fc1_weight_grad: float32 [2048, 8192], P('dp', 'tensor')
- fc1_bias_grad: float32 [4, 2048], P('tensor', 'dp')
- fc2_weight_grad: float32 [8192, 2048], P('tensor', 'dp')
- fc2_bias_grad: float32 [2048], P(('dp', 'tensor'))
All inputs are finite; a program needn't handle non-finite values. No bound on the sum of `keep_slot` on one device may be relied on, other than what follows from the above.
Results may differ from a plain program's by a relative error of at most 0.0092.
Values may be sent and summed in bfloat16 or wider, within the bound.
No kernel may reach another device: no remote copies, remote signals or barrier semaphores. Data moves between devices by JAX's collectives and lax.ppermute only.
A program may use at most 320 MiB of HBM per device.

v0:
```python
import math
import jax
import jax.numpy as jnp
from jax import lax
from jax.sharding import PartitionSpec as P

ROT = 64
layer_eps = 1e-05
rope_base = 10000.0
mask_fill = -1e30
block_rows = 512


def rope_tables(length, rot_dims):
    half = rot_dims // 2
    freqs = jnp.exp(-jnp.log(rope_base) * (2.0 * jnp.arange(half, dtype=jnp.float32) / rot_dims))
    angles = jnp.arange(length, dtype=jnp.float32)[:, None] * freqs[None, :]
    return (jnp.cos(angles), jnp.sin(angles))


def rotate(field, cosine, sine, rot_dims, sign):
    half = rot_dims // 2
    first = field[..., :half]
    second = field[..., half:rot_dims]
    rest = field[..., rot_dims:]
    cos_b = cosine[:, None, :]
    sin_b = sign * sine[:, None, :]
    return jnp.concatenate(
        [first * cos_b - second * sin_b, second * cos_b + first * sin_b, rest], axis=-1
    )


def gelu_exact(field):
    return jax.nn.gelu(field, approximate=False)


def contract_rows(left, right):
    return lax.dot_general(
        left, right, (((0,), (0,)), ((), ())), preferred_element_type=jnp.float32
    )


def contract_cols(left, right):
    return lax.dot_general(
        left, right, (((1,), (1,)), ((), ())), preferred_element_type=jnp.float32
    )


def local(
    hidden_in,
    keep_slot,
    out_grad,
    ln1_gain,
    ln1_bias,
    ln2_gain,
    ln2_bias,
    qkv_weight,
    qkv_bias,
    dense_weight,
    dense_bias,
    fc1_weight,
    fc1_bias,
    fc2_weight,
    fc2_bias,
):
    slot_count, own_len, width = hidden_in.shape
    seq_len = own_len * lax.axis_size("tensor")
    head_local, three_hd = qkv_bias.shape
    head_dim = three_hd // 3
    scale = 1.0 / math.sqrt(head_dim)
    start_row = lax.axis_index("tensor") * own_len
    inputs_all, grads_all = (
        lax.all_gather(hidden_in, "tensor", axis=1, tiled=True),
        lax.all_gather(out_grad, "tensor", axis=1, tiled=True),
    )
    cosine, sine = rope_tables(seq_len, ROT)
    blk = min(block_rows, seq_len)
    n_blocks = seq_len // blk
    key_pos = jnp.arange(seq_len)
    starts = jnp.arange(n_blocks) * blk
    qkv_acc = jnp.zeros(qkv_weight.shape, jnp.float32)
    dense_acc = jnp.zeros(dense_weight.shape, jnp.float32)
    up_acc = jnp.zeros(fc1_weight.shape, jnp.float32)
    down_acc = jnp.zeros(fc2_weight.shape, jnp.float32)
    qkv_bias_acc = jnp.zeros((head_local * three_hd,), jnp.float32)
    up_bias_acc = jnp.zeros(fc1_bias.shape, jnp.float32)
    gain_one_acc = jnp.zeros((width,), jnp.float32)
    shift_one_acc = jnp.zeros((width,), jnp.float32)
    gain_two_acc = jnp.zeros((width,), jnp.float32)
    shift_two_acc = jnp.zeros((width,), jnp.float32)
    out_bias_acc = jnp.zeros((width,), jnp.float32)
    out_rows = []
    grad_rows_out = []
    for slot_idx in range(slot_count):
        keep = keep_slot[slot_idx].astype(jnp.float32)
        rows_full = inputs_all[slot_idx].astype(jnp.float32)
        centred = rows_full - jnp.mean(rows_full, axis=-1, keepdims=True)
        inv_std = lax.rsqrt(jnp.mean(centred * centred, axis=-1, keepdims=True) + layer_eps)
        normed = centred * inv_std
        normed_one = (normed * ln1_gain + ln1_bias).astype(jnp.bfloat16)
        normed_two = (normed * ln2_gain + ln2_bias).astype(jnp.bfloat16)
        joined = jnp.dot(
            normed_one, qkv_weight, preferred_element_type=jnp.float32
        ) + qkv_bias.reshape(-1)
        joined = joined.reshape(seq_len, head_local, 3, head_dim)
        query_rot = rotate(joined[:, :, 0], cosine, sine, ROT, 1.0).astype(jnp.bfloat16)
        key_rot = rotate(joined[:, :, 1], cosine, sine, ROT, 1.0).astype(jnp.bfloat16)
        value_rows = joined[:, :, 2].astype(jnp.bfloat16)
        query_blocks = query_rot.reshape(n_blocks, blk, head_local, head_dim)

        def block_scores(query_blk, blk_start):
            scores = (
                jnp.einsum("bhd,khd->hbk", query_blk, key_rot, preferred_element_type=jnp.float32)
                * scale
            )
            allowed = key_pos[None, :] <= (blk_start + jnp.arange(blk))[:, None]
            return jnp.where(allowed[None], scores, mask_fill)

        def attend(items):
            query_blk, blk_start = items
            scores = block_scores(query_blk, blk_start)
            top = jnp.max(scores, axis=-1, keepdims=True)
            weights = jnp.exp(scores - top)
            total = jnp.sum(weights, axis=-1, keepdims=True)
            probs = weights / total
            mixed = jnp.einsum(
                "hbk,khd->bhd",
                probs.astype(jnp.bfloat16),
                value_rows,
                preferred_element_type=jnp.float32,
            )
            return (mixed.astype(jnp.bfloat16), (top + jnp.log(total))[..., 0])

        attn_blocks, log_total = lax.map(attend, (query_blocks, starts))
        attn_flat = attn_blocks.reshape(seq_len, head_local * head_dim)
        pre_act = jnp.dot(normed_two, fc1_weight, preferred_element_type=jnp.float32) + fc1_bias
        act_val, act_back = jax.vjp(gelu_exact, pre_act)
        act_low = act_val.astype(jnp.bfloat16)
        partial_out = jnp.dot(
            attn_flat, dense_weight, preferred_element_type=jnp.float32
        ) + jnp.dot(act_low, fc2_weight, preferred_element_type=jnp.float32)
        summed = lax.psum(partial_out, "tensor")
        branch_own = lax.dynamic_slice_in_dim(summed, start_row, own_len, 0)
        branch_own = branch_own + dense_bias + fc2_bias
        own_in = hidden_in[slot_idx].astype(jnp.float32)
        out_rows.append((own_in + keep * branch_own).astype(jnp.bfloat16))
        branch_grad = grads_all[slot_idx] * keep_slot[slot_idx].astype(jnp.bfloat16)
        own_cot = out_grad[slot_idx].astype(jnp.float32)
        out_bias_acc = out_bias_acc + jnp.sum(own_cot * keep, axis=0)
        down_acc = down_acc + contract_rows(act_low, branch_grad)
        dense_acc = dense_acc + contract_rows(attn_flat, branch_grad)
        act_grad = contract_cols(branch_grad, fc2_weight)
        pre_grad = act_back(act_grad)[0].astype(jnp.bfloat16)
        up_bias_acc = up_bias_acc + jnp.sum(pre_grad.astype(jnp.float32), axis=0)
        up_acc = up_acc + contract_rows(normed_two, pre_grad)
        normed_two_grad = contract_cols(pre_grad, fc1_weight)
        mixed_grad = contract_cols(branch_grad, dense_weight).astype(jnp.bfloat16)
        grad_blocks = mixed_grad.reshape(n_blocks, blk, head_local, head_dim)

        def attend_back(carry, items):
            key_acc, value_acc = carry
            query_blk, grad_blk, lse_blk, blk_start = items
            scores = block_scores(query_blk, blk_start)
            probs = jnp.exp(scores - lse_blk[..., None])
            probs_low = probs.astype(jnp.bfloat16)
            prob_grad = jnp.einsum(
                "bhd,khd->hbk", grad_blk, value_rows, preferred_element_type=jnp.float32
            )
            inner = jnp.sum(probs * prob_grad, axis=-1, keepdims=True)
            score_grad = (probs * (prob_grad - inner)).astype(jnp.bfloat16)
            query_grad = (
                jnp.einsum("hbk,khd->bhd", score_grad, key_rot, preferred_element_type=jnp.float32)
                * scale
            )
            key_acc = (
                key_acc
                + jnp.einsum(
                    "hbk,bhd->khd", score_grad, query_blk, preferred_element_type=jnp.float32
                )
                * scale
            )
            value_acc = value_acc + jnp.einsum(
                "hbk,bhd->khd", probs_low, grad_blk, preferred_element_type=jnp.float32
            )
            return ((key_acc, value_acc), query_grad)

        empty = jnp.zeros((seq_len, head_local, head_dim), jnp.float32)
        (key_grad, value_grad), query_grad = lax.scan(
            attend_back, (empty, empty), (query_blocks, grad_blocks, log_total, starts)
        )
        query_grad = rotate(
            query_grad.reshape(seq_len, head_local, head_dim), cosine, sine, ROT, -1.0
        )
        key_grad = rotate(key_grad, cosine, sine, ROT, -1.0)
        joined_grad = (
            jnp.stack([query_grad, key_grad, value_grad], axis=2)
            .reshape(seq_len, head_local * three_hd)
            .astype(jnp.bfloat16)
        )
        qkv_bias_acc = qkv_bias_acc + jnp.sum(joined_grad.astype(jnp.float32), axis=0)
        qkv_acc = qkv_acc + contract_rows(normed_one, joined_grad)
        normed_one_grad = contract_cols(joined_grad, qkv_weight)
        gain_one_acc = gain_one_acc + jnp.sum(normed_one_grad * normed, axis=0)
        shift_one_acc = shift_one_acc + jnp.sum(normed_one_grad, axis=0)
        gain_two_acc = gain_two_acc + jnp.sum(normed_two_grad * normed, axis=0)
        shift_two_acc = shift_two_acc + jnp.sum(normed_two_grad, axis=0)
        normed_grad = normed_one_grad * ln1_gain + normed_two_grad * ln2_gain
        grad_summed = lax.psum(normed_grad.astype(jnp.bfloat16), "tensor").astype(jnp.float32)
        own_grad = lax.dynamic_slice_in_dim(grad_summed, start_row, own_len, 0)
        own_normed = lax.dynamic_slice_in_dim(normed, start_row, own_len, 0)
        own_inv = lax.dynamic_slice_in_dim(inv_std, start_row, own_len, 0)
        back_rows = own_inv * (
            own_grad
            - jnp.mean(own_grad, axis=-1, keepdims=True)
            - own_normed * jnp.mean(own_grad * own_normed, axis=-1, keepdims=True)
        )
        grad_rows_out.append(own_cot + back_rows)
    weight_parts = (
        lax.psum_scatter(qkv_acc, "dp", scatter_dimension=0, tiled=True),
        lax.psum_scatter(dense_acc, "dp", scatter_dimension=1, tiled=True),
        lax.psum_scatter(up_acc, "dp", scatter_dimension=0, tiled=True),
        lax.psum_scatter(down_acc, "dp", scatter_dimension=1, tiled=True),
        lax.psum_scatter(
            qkv_bias_acc.reshape(head_local, three_hd), "dp", scatter_dimension=1, tiled=True
        ),
        lax.psum_scatter(up_bias_acc.reshape(1, -1), "dp", scatter_dimension=1, tiled=True),
    )
    small_parts = lax.psum_scatter(
        jnp.stack([gain_one_acc, shift_one_acc, gain_two_acc, shift_two_acc, out_bias_acc]),
        ("dp", "tensor"),
        scatter_dimension=1,
        tiled=True,
    )
    block_out = jnp.stack(out_rows)
    hidden_grad = jnp.stack(grad_rows_out)
    return (
        block_out,
        hidden_grad,
        small_parts[0],
        small_parts[1],
        small_parts[2],
        small_parts[3],
        weight_parts[0],
        weight_parts[4],
        weight_parts[1],
        small_parts[4],
        weight_parts[2],
        weight_parts[5],
        weight_parts[3],
        small_parts[4],
    )


def solution(mesh):
    in_specs = (
        P("dp", "tensor", None),
        P("dp"),
        P("dp", "tensor", None),
        P(),
        P(),
        P(),
        P(),
        P(None, "tensor"),
        P("tensor", None),
        P("tensor", None),
        P(),
        P(None, "tensor"),
        P("tensor"),
        P("tensor", None),
        P(),
    )
    out_specs = (
        P("dp", "tensor", None),
        P("dp", "tensor", None),
        P(("dp", "tensor")),
        P(("dp", "tensor")),
        P(("dp", "tensor")),
        P(("dp", "tensor")),
        P("dp", "tensor"),
        P("tensor", "dp"),
        P("tensor", "dp"),
        P(("dp", "tensor")),
        P("dp", "tensor"),
        P("tensor", "dp"),
        P("tensor", "dp"),
        P(("dp", "tensor")),
    )
    return jax.shard_map(local, mesh=mesh, in_specs=in_specs, out_specs=out_specs, check_vma=False)
```

profile of v0, /device:TPU:0, one launch (start us, length us, event | category | flops | bytes accessed | tf_op | source)
XLA Modules:
  0.0 2166.4 jit_solution(5631583935324290304)
XLA Ops:
  13.9 148.1 %all-gather.3.cloned.1.call-done = bf16[2,1024,2048]{2,1,0:T(8,128)(2,1)} async-done(((bf16[2,256,2048]{2,1,0:T(8,128)(2,1)}), bf16[2,1024,2048]{2,1,0:T(8,128)(2,1)}) %all-gather.3.cloned.1.call-update) | async-done | bytes 8388624 | tf_op jit(solution)/shard_map/all_gather | solution.py:73
  171.5 8.9 convolution_add_fusion.4
  180.4 6.6 copy.95
  187.7 12.4 convolution_add_fusion.3
  200.0 6.6 copy.103
  236.9 17.1 while.57
  254.0 57.4 %all-gather.5.cloned.1.call-done = bf16[2,1024,2048]{2,1,0:T(8,128)(2,1)} async-done(((bf16[2,256,2048]{2,1,0:T(8,128)(2,1)}), bf16[2,1024,2048]{2,1,0:T(8,128)(2,1)}) %all-gather.5.cloned.1.call-update) | async-done | bytes 8388624 | tf_op jit(solution)/shard_map/all_gather | solution.py:74
  311.4 5.5 convolution_convert_fusion
  319.1 41.9 %while.59 = (s32[]{:T(128)}, f32[1024,2,256]{0,2,1:T(8,128)}, f32[1024,2,256]{0,2,1:T(8,128)}, f32[2,512,2,256]{3,1,0,2:T(8,128)}, bf16[2,512,2,256]{3,1,2,0:T(8...) while((s32[]{:T(128)}, f32[1024,2,256]{0,2,1:T(8,128)}, ...), condition=%wide.region_22.23_spmd.clone, body=%wide.region_20.22_spmd.clone.sunk | while | flops 2703490560 | bytes 112231744 | solution.py:188
  348.6 4.7 bitcast_add_fusion.10
  356.5 4.5 bitcast_add_fusion.11
  385.5 15.8 while.56
  401.3 5.5 convolution_convert_fusion.1
  408.9 82.9 %while.58 = (s32[]{:T(128)}, f32[1024,2,256]{0,2,1:T(8,128)}, f32[1024,2,256]{0,2,1:T(8,128)}, f32[2,512,2,256]{1,0,3,2:T(2,128)}, bf16[2,512,2,256]{3,1,2,0:T(8...) while((s32[]{:T(128)}, f32[1024,2,256]{0,2,1:T(8,128)}, ...), condition=%wide.region_16.17_spmd.clone, body=%wide.region_14.16_spmd.clone.sunk | while | flops 2703490560 | bytes 112231848 | solution.py:188
  422.7 19.6 dynamic_update_slice.42
  463.1 19.6 dynamic_update_slice.42
  482.6 4.6 bitcast_add_fusion.8
  487.3 4.5 bitcast_add_fusion.9
  529.6 4.7 copy.129
  534.3 11.9 fusion.170
  546.3 10.9 fusion.172
  557.3 11.8 fusion.162
  569.2 50.6 %multiply_convert_fusion.3 = (bf16[1024,2048]{1,0:T(8,128)(2,1)}, f32[1024,2048]{1,0:T(8,128)}, bf16[1024,2048]{1,0:T(8,128)(2,1)}, f32[1024,2048]{1,0:T(8,128)}, f32[1024,2048]{1,0:T(8,128)}) fusion(f32[2048]{0:T(1024)S(1)} %copy-done.52, f32[1024,2048]{1,0:T(8,128)} %fusion.162, bf16[2048,2048]{1,0:T(8,128)(2,1)S(1)} %bitcast.409, ...), kind=kOutput, calls=%fused_computation.149 | convolution fusion | flops 8879341568 | bytes 54558720 | tf_op jit(solution)/shard_map/dot_general | solution.py:136
  619.7 19.0 convert_reduce_fusion.3
  638.7 14.8 fusion.171
  653.5 20.4 convert_reduce_fusion.2
  673.9 29.7 %multiply_reduce_fusion.2 = (f32[2048]{0:T(1024)S(1)}, f32[2048]{0:T(1024)S(1)}, f32[2048]{0:T(1024)S(1)}, f32[2048]{0:T(1024)S(1)}, f32[2048]{0:T(1024)S(1)}, /...) fusion(f32[1024]{0:T(1024)S(1)} %copy-done.55, ...), kind=kOutput, calls=%fused_computation.126 | convolution fusion | flops 8644444160 | bytes 71401472 | tf_op jit(solution)/shard_map/dot_general | solution.py:44
  706.0 15.5 fusion.168
  721.6 14.7 fusion.169
  740.5 9.4 convolution_add_fusion.6
  749.9 242.9 %all-reduce.7.cloned.1.call-done = (bf16[1024,2048]{1,0:T(8,128)(2,1)}, bf16[1024,2048]{1,0:T(8,128)(2,1)}) async-done(((bf16[1024,2048]{1,0:T(8,128)(2,1)}, bf16[1024,2048]{1,0:T(8,128)(2,1)}), (bf16[1024,2048]{1,0:T(8,128)(2,1)}, bf16[1024,2048]{1,0:T(8,128)(2,1)})) %all-reduce.7.cloned.1.call-update) | async-done | bytes 8388624 | tf_op jit(solution)/shard_map/psum | solution.py:208
  997.8 5.1 fusion.125
  1004.9 9.1 convolution_add_fusion.5
  1014.0 4.9 fusion.136
  1018.9 6.5 convolution_add_fusion.7
  1026.1 14.5 fusion.102
  1040.7 16.0 convolution_add_fusion
  1057.4 15.9 fusion.160
  1073.3 17.9 convolution_add_fusion.2
  1091.5 15.4 fusion.134
  1106.9 17.1 convolution_add_fusion.1
  1127.8 4.7 pad_maximum_fusion
  1132.5 74.2 %reduce-scatter.22.cloned.1.call-done = f32[64,5]{1,0:T(8,128)} async-done(((f32[2048,5]{1,0:T(8,128)}), f32[64,5]{1,0:T(8,128)}) %reduce-scatter.22.cloned.1.call-update) | async-done | bytes 1296
  1210.3 557.9 %all-reduce.5.cloned.1.call-done = (f32[1024,2048]{1,0:T(8,128)}, f32[1024,2048]{1,0:T(8,128)}) async-done(((f32[1024,2048]{1,0:T(8,128)}, f32[1024,2048]{1,0:T(8,128)}), (f32[1024,2048]{1,0:T(8,128)}, f32[1024,2048]{1,0:T(8,128)})) %all-reduce.5.cloned.1.call-update) | async-done | bytes 16777232 | tf_op jit(solution)/shard_map/psum | solution.py:142
  1773.5 48.7 %reduce-scatter.16.cloned.1.call-done = f32[512,256]{1,0:T(8,128)} async-done(((f32[512,2048]{1,0:T(8,128)}), f32[512,256]{1,0:T(8,128)}) %reduce-scatter.16.cloned.1.call-update) | async-done | bytes 524304 | tf_op jit(solution)/shard_map/reduce_scatter | solution.py:220
  1822.2 96.4 %reduce-scatter.14.cloned.1.call-done = f32[256,1536]{1,0:T(8,128)} async-done(((f32[2048,1536]{1,0:T(8,128)}), f32[256,1536]{1,0:T(8,128)}) %reduce-scatter.14.cloned.1.call-update) | async-done | bytes 1572880 | tf_op jit(solution)/shard_map/reduce_scatter | solution.py:219
  1918.6 120.2 %reduce-scatter.18.cloned.1.call-done = f32[256,2048]{1,0:T(8,128)} async-done(((f32[2048,2048]{1,0:T(8,128)}), f32[256,2048]{1,0:T(8,128)}) %reduce-scatter.18.cloned.1.call-update) | async-done | bytes 2097168 | tf_op jit(solution)/shard_map/reduce_scatter | solution.py:221
  2038.8 120.2 %reduce-scatter.20.cloned.1.call-done = f32[2048,256]{1,0:T(8,128)} async-done(((f32[2048,2048]{1,0:T(8,128)}), f32[2048,256]{1,0:T(8,128)}) %reduce-scatter.20.cloned.1.call-update) | async-done | bytes 2097168 | tf_op jit(solution)/shard_map/reduce_scatter | solution.py:222
  (401 shorter events, 237.9 us)
Async XLA Ops:
  7.2 304.2 %copy-start = (bf16[512,2048]{1,0:T(8,128)(2,1)S(1)}, bf16[512,2048]{1,0:T(8,128)(2,1)}, u32[]{:S(2)}) copy-start(bf16[512,2048]{1,0:T(8,128)(2,1)} %param.32) | copy-start | bytes 6291460
  7.2 5.4 copy-start.61
  7.3 6.0 copy-start.62
  7.3 154.7 %all-gather.3.cloned.1.call-start = ((), (), s32[]{:S(2)}) async-start(), calls=%async_computation.7 | async-start | bytes 10485760 | tf_op jit(solution)/shard_map/all_gather | solution.py:73
  8.0 303.4 %all-gather.5.cloned.1.call-start = ((), (), s32[]{:S(2)}) async-start(), calls=%async_computation.8 | async-start | bytes 10485760 | tf_op jit(solution)/shard_map/all_gather | solution.py:74
  8.8 984.1 %all-reduce.7.cloned.1.call-start = ((), (), s32[]{:S(2)}) async-start(), calls=%async_computation.17 | async-start | bytes 16777216 | tf_op jit(solution)/shard_map/psum | solution.py:208
  8.9 178.1 %copy-start.48 = (f32[2048]{0:T(1024)}, f32[2048]{0:T(1024)S(1)}, u32[]{:S(2)}) copy-start(f32[2048]{0:T(1024)S(1)} %convert_element_type.255) | copy-start | bytes 24580
  8.9 178.1 %copy-start.50 = (f32[2048]{0:T(1024)}, f32[2048]{0:T(1024)S(1)}, u32[]{:S(2)}) copy-start(f32[2048]{0:T(1024)S(1)} %convert_element_type.256) | copy-start | bytes 24580
  10.2 203.0 %copy-start.33 = (f32[1024,32]{0,1:T(8,128)}, f32[1024,32]{0,1:T(8,128)S(1)}, u32[]{:S(2)}) copy-start(f32[1024,32]{0,1:T(8,128)S(1)} %get-tuple-element.592) | copy-start | bytes 393220
  162.0 5.9 copy-start.13
  166.3 20.8 copy-start.40
  254.0 63.0 %copy-start.22 = (bf16[2,512,2,256]{3,2,1,0:T(2,128)(2,1)}, bf16[2,512,2,256]{3,2,1,0:T(2,128)(2,1)S(1)}, u32[]{:S(2)}) copy-start(bf16[2,512,2,256]{3,2,1,0:T(2,128)(2,1)S(1)} %get-tuple-element.219) | copy-start | bytes 3145732
  328.9 7.3 copy-start.4
  348.6 7.9 copy-start.4
  491.8 5.7 copy-start.24
  495.9 9.2 copy-start.34
  507.8 10.9 copy-start.37
  511.7 8.4 copy-start.35
  511.7 8.4 copy-start.36
  534.3 11.9 copy-start.25
  534.3 22.9 %slice-start = ((s8[8388608]{0:T(1024)(128)(4,1)}), s8[4194304]{0:T(1024)(128)(4,1)S(1)}, s32[]{:S(2)}) async-start(s8[8388608]{0:T(1024)(128)(4,1)} %bitcast.368), calls=%async_computation.18 | async-start | bytes 8388608
  534.3 22.9 %slice-start.4 = ((s8[8388608]{0:T(1024)(128)(4,1)}), s8[4194304]{0:T(1024)(128)(4,1)S(1)}, s32[]{:S(2)}) async-start(s8[8388608]{0:T(1024)(128)(4,1)} %bitcast.408), calls=%async_computation.22 | async-start | bytes 8388608
  546.2 11.0 slice-start.1
  546.2 11.0 slice-start.5
  546.2 11.0 copy-start.41
  546.3 11.0 copy-start.45
  546.3 11.0 copy-start.46
  546.3 11.0 copy-start.54
  557.3 11.9 copy-start.44
  557.3 11.9 copy-start.52
  557.3 11.9 copy-start.57
  638.7 14.8 copy-start.71
  653.5 20.4 copy-start.42
  653.5 20.4 copy-start.49
  653.5 20.4 copy-start.55
  703.6 421.1 %reduce-scatter.24.cloned.1.call-start = ((), (), s32[]{:S(2)}) async-start(), calls=%async_computation.14 | async-start | bytes 442368
  721.5 404.7 %reduce-scatter.26.cloned.1.call-start = ((), (), s32[]{:S(2)}) async-start(), calls=%async_computation.15 | async-start | bytes 1179648
  721.6 17.3 copy-start.23
  740.5 466.3 %reduce-scatter.22.cloned.1.call-start = ((), (), s32[]{:S(2)}) async-start(), calls=%async_computation.13 | async-start | bytes 1081344
  1004.4 763.8 %all-reduce.5.cloned.1.call-start = ((), (), s32[]{:S(2)}) async-start(), calls=%async_computation.16 | async-start | bytes 33554432 | tf_op jit(solution)/shard_map/psum | solution.py:142
  1014.0 808.2 %reduce-scatter.16.cloned.1.call-start = ((), (), s32[]{:S(2)}) async-start(), calls=%async_computation.10 | async-start | bytes 4718592 | tf_op jit(solution)/shard_map/reduce_scatter | solution.py:220
  1025.5 893.1 %reduce-scatter.14.cloned.1.call-start = ((), (), s32[]{:S(2)}) async-start(), calls=%async_computation.9 | async-start | bytes 14155776 | tf_op jit(solution)/shard_map/reduce_scatter | solution.py:219
  1026.1 14.5 copy-start.26
  1056.7 982.0 %reduce-scatter.18.cloned.1.call-start = ((), (), s32[]{:S(2)}) async-start(), calls=%async_computation.11 | async-start | bytes 18874368 | tf_op jit(solution)/shard_map/reduce_scatter | solution.py:221
  1057.4 15.9 copy-start.70
  1091.2 1067.7 %reduce-scatter.20.cloned.1.call-start = ((), (), s32[]{:S(2)}) async-start(), calls=%async_computation.12 | async-start | bytes 18874368 | tf_op jit(solution)/shard_map/reduce_scatter | solution.py:222
  1091.5 15.4 copy-start.69
  1207.9 951.0 %copy-start.67 = (f32[1,64]{1,0:T(1,128)}, f32[1,64]{1,0:T(1,128)S(1)}, u32[]{:S(2)}) copy-start(f32[1,64]{1,0:T(1,128)S(1)} %copy.159) | copy-start | bytes 772
  (57 other events, 175.1 us)
Sparse Core Ops, SparseCore 0:
  9.6 152.3 all-gather.2
  163.6 147.7 all-gather.4
  703.8 289.0 all-reduce.6
  995.7 32.8 reduce-scatter.23
  1031.7 35.9 reduce-scatter.25
  1069.8 136.9 reduce-scatter.21
  1209.4 558.7 all-reduce.4
  1772.1 49.9 reduce-scatter.15
  1826.2 92.3 reduce-scatter.13
  1922.6 116.1 reduce-scatter.17
  2042.9 115.9 reduce-scatter.19
where the time goes:
time: 2180 us; the launch traced here: 2170 us
  waiting for transfers between devices  1470 us (67%)
  matrix products  433 us (20%)
  local copies, waits for them, and re-layouts  175 us (8%)
  other arithmetic  70 us (3%)
    psum x1, waiting for transfers between devices, local(): summed = lax.psum(partial_out, 'tensor')  558 us
    psum x1, waiting for transfers between devices, local(): lax.psum(normed_grad.astype(jnp.bfloat16), 'tensor').astype(jnp.float32)  243 us
    all_gather x1, waiting for transfers between devices, local(): lax.all_gather(hidden_in, 'tensor', axis=1, tiled=True)  148 us
    reduce_scatter x1, waiting for transfers between devices, local(): lax.psum_scatter(up_acc, 'dp', scatter_dimension=0, tiled=True)  120 us
    reduce_scatter x1, waiting for transfers between devices, local(): lax.psum_scatter(down_acc, 'dp', scatter_dimension=1, tiled=True)  120 us
    dot_general x8, matrix products, contract_cols(): lax.dot_general(left, right, (((1,), (1,)), ((), ())), preferred_element_...  118 us
    dot_general x8, matrix products, contract_rows(): lax.dot_general(left, right, (((0,), (0,)), ((), ())), preferred_element_...  108 us
    reduce_scatter x1, waiting for transfers between devices, local(): lax.psum_scatter(qkv_acc, 'dp', scatter_dimension=0, tiled=True)  96.4 us
  transfers between devices with their start and end apart: 11, of which 9 were waited for; matrix products, arithmetic and copies ran while one was open for 13% of the time, Pallas kernels for 0%

commit v1 on v0

--- a/solution.py
+++ b/solution.py
@@ -9,6 +9,28 @@
 rope_base = 10000.0
 mask_fill = -1e30
 block_rows = 512
+
+
+def laid_out(tiles, dim):
+    tiles = jnp.moveaxis(tiles, 0, dim)
+    shape = tiles.shape
+    return tiles.reshape(*shape[:dim], shape[dim] * shape[dim + 1], *shape[dim + 2 :])
+
+
+def doubled(x, axis):
+    length = lax.axis_size(axis)
+    blocks = x[None]
+    for level in range(length.bit_length() - 1):
+        bit = 1 << level
+        other = lax.ppermute(blocks, axis, [(i, i ^ bit) for i in range(length)])
+        both = jnp.stack([blocks, other])
+        upper = lax.axis_index(axis) >> level & 1
+        blocks = jnp.where(upper == 0, both, both[::-1]).reshape(-1, *x.shape)
+    return blocks
+
+
+def doubled_up(array, axis, dim):
+    return laid_out(doubled(array, axis), dim)
 
 
 def rope_tables(length, rot_dims):
@@ -70,7 +92,7 @@
     scale = 1.0 / math.sqrt(head_dim)
     start_row = lax.axis_index("tensor") * own_len
     inputs_all, grads_all = (
-        lax.all_gather(hidden_in, "tensor", axis=1, tiled=True),
+        doubled_up(hidden_in, "tensor", 1),
         lax.all_gather(out_grad, "tensor", axis=1, tiled=True),
     )
     cosine, sine = rope_tables(seq_len, ROT)

time: 2180 us -> 2390 us (1.096)
  waiting for transfers between devices: 1470 us -> 1630 us
  other arithmetic: 70 us -> 117 us
  matrix products: 433 us -> 407 us
    ppermute x0 -> x2, waiting for transfers between devices: none -> 357 us  [doubled(): other = lax.ppermute(blocks, axis, [(i, i ^ bit) for i in range(length)])]
    all_gather x1 -> x0, waiting for transfers between devices: 148 us -> none  [local(): lax.all_gather(hidden_in, 'tensor', axis=1, tiled=True)]
    all_gather x1, waiting for transfers between devices: 57.4 us -> 0.01 us  [local(): lax.all_gather(out_grad, 'tensor', axis=1, tiled=True)]
    unnamed x14 -> x13, waiting for transfers between devices: 75.8 us -> 79.5 us
  transfers between devices with their start and end apart: 11 -> 12, of which waited for: 9 -> 9; matrix products, arithmetic and copies ran while one was open for 13% -> 18% of each run, Pallas kernels for 0% -> 0%
where the time goes in v1:
time: 2390 us; the launch traced here: 2380 us
  waiting for transfers between devices  1630 us (68%)
  matrix products  407 us (17%)
  local copies, waits for them, and re-layouts  194 us (8%)
  other arithmetic  117 us (5%)
    psum x1, waiting for transfers between devices, local(): summed = lax.psum(partial_out, 'tensor')  558 us
    ppermute x2, waiting for transfers between devices, doubled(): other = lax.ppermute(blocks, axis, [(i, i ^ bit) for i in range(length)])  357 us
    psum x1, waiting for transfers between devices, local(): lax.psum(normed_grad.astype(jnp.bfloat16), 'tensor').astype(jnp.float32)  253 us
    reduce_scatter x1, waiting for transfers between devices, local(): lax.psum_scatter(up_acc, 'dp', scatter_dimension=0, tiled=True)  120 us
    reduce_scatter x1, waiting for transfers between devices, local(): lax.psum_scatter(down_acc, 'dp', scatter_dimension=1, tiled=True)  120 us
    dot_general x8, matrix products, contract_cols(): lax.dot_general(left, right, (((1,), (1,)), ((), ())), preferred_element_...  115 us
    dot_general x8, matrix products, contract_rows(): lax.dot_general(left, right, (((0,), (0,)), ((), ())), preferred_element_...  98.5 us
    reduce_scatter x1, waiting for transfers between devices, local(): lax.psum_scatter(qkv_acc, 'dp', scatter_dimension=0, tiled=True)  96.4 us
  transfers between devices with their start and end apart: 12, of which 9 were waited for; matrix products, arithmetic and copies ran while one was open for 18% of the time, Pallas kernels for 0%

profile of v1, /device:TPU:0, one launch (start us, length us, event | category | flops | bytes accessed | tf_op | source)
XLA Modules:
  0.0 2377.6 jit_solution(2246316840383940598)
XLA Ops:
  10.4 45.9 %collective-permute-done = bf16[1,2,256,2048]{3,2,1,0:T(8,128)(2,1)} collective-permute-done((bf16[1,2,256,2048]{3,2,1,0:T(8,128)(2,1)}, bf16[1,2,256,2048]{3,2,1,0:T(8,128)(2,1)}, u32[]{:S(2)}, u32[]{:S(2)}) %collective-permute-start) | collective-permute-done | bytes 2097184 | tf_op jit(solution)/shard_map/ppermute | solution.py:25
  59.0 4.9 fusion.88
  70.7 311.0 %collective-permute-done.1 = bf16[2,2,256,2048]{3,2,1,0:T(8,128)(2,1)} collective-permute-done((bf16[2,2,256,2048]{3,2,1,0:T(8,128)(2,1)}, bf16[2,2,256,2048]{3,2,1,0:T(8,128)(2,1)}, u32[]{:S(2)}, u32[]{:S(2)}) %collective-permute-start.1) | collective-permute-done | bytes 4194336 | tf_op jit(solution)/shard_map/ppermute | solution.py:25
  381.7 7.5 pad_maximum_fusion
  389.2 14.2 reverse_select_fusion
  403.4 8.3 copy_bitcast_fusion.6
  421.4 9.1 add_convert_fusion.8
  430.5 10.5 convolution_add_fusion.4
  441.0 6.6 copy.98
  447.6 5.0 slice_bitcast_fusion.2
  455.3 10.5 convolution_add_fusion.3
  465.8 6.6 copy.106
  502.9 15.6 while.56
  541.8 16.1 while.57
  557.9 12.6 fusion.135
  573.8 48.6 %multiply_convert_fusion.3 = (bf16[1024,2048]{1,0:T(8,128)(2,1)}, f32[1024,2048]{1,0:T(8,128)}, bf16[1024,2048]{1,0:T(8,128)(2,1)}, f32[1024,2048]{1,0:T(8,128)}, f32[1024,2048]{1,0:T(8,128)}) fusion(f32[2048]{0:T(1024)S(1)} %copy-done.74, f32[1024,2048]{1,0:T(8,128)S(1)} %fusion.135, bf16[1024,2048]{1,0:T(8,128)(2,1)S(1)} %copy-done.28, ...), kind=kOutput, calls=%fused_computation.137 | convolution fusion | flops 8866758656 | bytes 54534144 | tf_op jit(solution)/shard_map/dot_general | solution.py:158
  628.1 40.3 %while.59 = (s32[]{:T(128)}, f32[1024,2,256]{0,2,1:T(8,128)}, f32[1024,2,256]{0,2,1:T(8,128)}, f32[2,512,2,256]{3,1,0,2:T(8,128)}, bf16[2,512,2,256]{3,1,2,0:T(8...) while((s32[]{:T(128)}, f32[1024,2,256]{0,2,1:T(8,128)}, ...), condition=%wide.region_22.23_spmd.clone, body=%wide.region_20.22_spmd.clone.sunk | while | flops 2703490560 | bytes 116426080 | solution.py:210
  673.1 5.6 convolution_convert_fusion.1
  680.9 83.7 %while.58 = (s32[]{:T(128)}, f32[1024,2,256]{0,2,1:T(8,128)}, f32[1024,2,256]{0,2,1:T(8,128)}, f32[2,512,2,256]{1,0,3,2:T(2,128)}, bf16[2,512,2,256]{3,1,2,0:T(8...) while((s32[]{:T(128)}, f32[1024,2,256]{0,2,1:T(8,128)}, ...), condition=%wide.region_16.17_spmd.clone, body=%wide.region_14.16_spmd.clone.sunk | while | flops 2703490560 | bytes 112231848 | solution.py:210
  695.0 19.6 dynamic_update_slice.42
  735.6 19.6 dynamic_update_slice.42
  807.0 12.1 fusion.137
  819.1 10.9 fusion.139
  830.0 19.2 convert_reduce_fusion.1
  849.2 14.9 fusion.138
  864.1 20.3 convert_reduce_fusion
  884.4 27.5 %multiply_reduce_fusion.2 = (f32[2048]{0:T(1024)S(1)}, f32[2048]{0:T(1024)S(1)}, f32[2048]{0:T(1024)S(1)}, f32[2048]{0:T(1024)S(1)}, f32[2048]{0:T(1024)S(1)}, /...) fusion(f32[1024]{0:T(1024)S(1)} %bitcast.422, ...), kind=kOutput, calls=%fused_computation.113 | convolution fusion | flops 8644444160 | bytes 63012864 | tf_op jit(solution)/shard_map/dot_general | solution.py:66
  914.8 12.8 fusion.134
  927.7 5.6 convolution_add_fusion.6
  933.3 13.4 fusion.136
  950.7 253.2 %all-reduce.7.cloned.1.call-done = (bf16[1024,2048]{1,0:T(8,128)(2,1)}, bf16[1024,2048]{1,0:T(8,128)(2,1)}) async-done(((bf16[1024,2048]{1,0:T(8,128)(2,1)}, bf16[1024,2048]{1,0:T(8,128)(2,1)}), (bf16[1024,2048]{1,0:T(8,128)(2,1)}, bf16[1024,2048]{1,0:T(8,128)(2,1)})) %all-reduce.7.cloned.1.call-update) | async-done | bytes 8388624 | tf_op jit(solution)/shard_map/psum | solution.py:230
  1209.0 5.1 fusion.92
  1215.8 9.0 convolution_add_fusion.5
  1224.9 4.9 fusion.103
  1229.8 6.6 convolution_add_fusion.7
  1237.1 5.6 add_convert_fusion
  1242.7 9.6 fusion.140
  1252.3 13.2 convolution_add_fusion
  1265.7 15.5 fusion.141
  1281.3 16.0 convolution_add_fusion.2
  1297.6 15.5 fusion.101
  1313.1 17.3 convolution_add_fusion.1
  1338.8 79.3 %reduce-scatter.22.cloned.1.call-done = f32[64,5]{1,0:T(8,128)} async-done(((f32[2048,5]{1,0:T(8,128)}), f32[64,5]{1,0:T(8,128)}) %reduce-scatter.22.cloned.1.call-update) | async-done | bytes 1296
  1421.6 557.7 %all-reduce.5.cloned.1.call-done = (f32[1024,2048]{1,0:T(8,128)}, f32[1024,2048]{1,0:T(8,128)}) async-done(((f32[1024,2048]{1,0:T(8,128)}, f32[1024,2048]{1,0:T(8,128)}), (f32[1024,2048]{1,0:T(8,128)}, f32[1024,2048]{1,0:T(8,128)})) %all-reduce.5.cloned.1.call-update) | async-done | bytes 16777232 | tf_op jit(solution)/shard_map/psum | solution.py:164
  1984.5 48.7 %reduce-scatter.16.cloned.1.call-done = f32[512,256]{1,0:T(8,128)} async-done(((f32[512,2048]{1,0:T(8,128)}), f32[512,256]{1,0:T(8,128)}) %reduce-scatter.16.cloned.1.call-update) | async-done | bytes 524304 | tf_op jit(solution)/shard_map/reduce_scatter | solution.py:242
  2033.2 96.4 %reduce-scatter.14.cloned.1.call-done = f32[256,1536]{1,0:T(8,128)} async-done(((f32[2048,1536]{1,0:T(8,128)}), f32[256,1536]{1,0:T(8,128)}) %reduce-scatter.14.cloned.1.call-update) | async-done | bytes 1572880 | tf_op jit(solution)/shard_map/reduce_scatter | solution.py:241
  2129.7 120.3 %reduce-scatter.18.cloned.1.call-done = f32[256,2048]{1,0:T(8,128)} async-done(((f32[2048,2048]{1,0:T(8,128)}), f32[256,2048]{1,0:T(8,128)}) %reduce-scatter.18.cloned.1.call-update) | async-done | bytes 2097168 | tf_op jit(solution)/shard_map/reduce_scatter | solution.py:243
  2250.0 120.0 %reduce-scatter.20.cloned.1.call-done = f32[2048,256]{1,0:T(8,128)} async-done(((f32[2048,2048]{1,0:T(8,128)}), f32[2048,256]{1,0:T(8,128)}) %reduce-scatter.20.cloned.1.call-update) | async-done | bytes 2097168 | tf_op jit(solution)/shard_map/reduce_scatter | solution.py:244
  (444 shorter events, 281.5 us)
Async XLA Ops:
  7.2 615.3 %copy-start = (bf16[512,2048]{1,0:T(8,128)(2,1)S(1)}, bf16[512,2048]{1,0:T(8,128)(2,1)}, u32[]{:S(2)}) copy-start(bf16[512,2048]{1,0:T(8,128)(2,1)} %param.32) | copy-start | bytes 6291460
  7.2 615.2 %all-gather.2.cloned.1.call-start = ((), (), s32[]{:S(2)}) async-start(), calls=%async_computation.7 | async-start | bytes 10485760 | tf_op jit(solution)/shard_map/all_gather | solution.py:96
  7.2 49.1 %collective-permute-start = (bf16[1,2,256,2048]{3,2,1,0:T(8,128)(2,1)}, bf16[1,2,256,2048]{3,2,1,0:T(8,128)(2,1)}, u32[]{:S(2)}, u32[]{:S(2)}) collective-permute-start(bf16[1,2,256,2048]{3,2,1,0:T(8,128)(2,1)} %bitcast.392), channel_id=1, source_target_pairs={{0,1},{1,0},{2,3},{3,2},{4,5},{5,4},{6,7},{7,6},{8,9},{9,8},{10,11... | collective-permute-start | bytes 6291464 | tf_op jit(solution)/shard_map/ppermute | solution.py:25
  59.0 8.5 copy-start.84
  59.0 10.4 copy-start.83
  63.9 317.7 %collective-permute-start.1 = (bf16[2,2,256,2048]{3,2,1,0:T(8,128)(2,1)}, bf16[2,2,256,2048]{3,2,1,0:T(8,128)(2,1)}, u32[]{:S(2)}, u32[]{:S(2)}) collective-permute-start(bf16[2,2,256,2048]{3,2,1,0:T(8,128)(2,1)} %get-tuple-element.558), channel_id=1, source_target_pairs={{0,2},{1,3},{2,0},{3,1},{4,6},{5,7},{6,4},{7,5},{8,10},{9,11},{10,... | collective-permute-start | bytes 12582920 | tf_op jit(solution)/shard_map/ppermute | solution.py:25
  66.7 1137.3 %all-reduce.7.cloned.1.call-start = ((), (), s32[]{:S(2)}) async-start(), calls=%async_computation.16 | async-start | bytes 16777216 | tf_op jit(solution)/shard_map/psum | solution.py:230
  66.8 354.5 %copy-start.50 = (f32[2048]{0:T(1024)}, f32[2048]{0:T(1024)S(1)}, u32[]{:S(2)}) copy-start(f32[2048]{0:T(1024)S(1)} %convert_element_type.264) | copy-start | bytes 24580
  66.9 354.5 %copy-start.52 = (f32[2048]{0:T(1024)}, f32[2048]{0:T(1024)S(1)}, u32[]{:S(2)}) copy-start(f32[2048]{0:T(1024)S(1)} %convert_element_type.265) | copy-start | bytes 24580
  66.9 354.5 %copy-start.58 = (f32[2048]{0:T(1024)}, f32[2048]{0:T(1024)S(1)}, u32[]{:S(2)}) copy-start(f32[2048]{0:T(1024)S(1)} %convert_element_type.270) | copy-start | bytes 24580
  70.7 410.3 %copy-start.41 = (f32[1024,32]{0,1:T(8,128)}, f32[1024,32]{0,1:T(8,128)S(1)}, u32[]{:S(2)}) copy-start(f32[1024,32]{0,1:T(8,128)S(1)} %get-tuple-element.612) | copy-start | bytes 393220
  420.7 9.8 copy-start.62
  421.3 9.1 copy-start.64
  421.3 9.1 copy-start.66
  421.3 9.1 copy-start.68
  518.5 15.7 copy-start.8
  557.9 12.6 copy-start.46
  557.9 12.6 copy-start.86
  557.9 15.9 copy-start.28
  557.9 15.9 copy-start.74
  768.6 9.2 copy-start.42
  780.6 10.9 copy-start.45
  784.5 8.4 copy-start.44
  807.0 12.1 copy-start.34
  819.1 10.9 copy-start.75
  849.2 14.9 copy-start.92
  864.1 20.3 copy-start.51
  864.1 20.3 copy-start.59
  864.1 20.3 copy-start.63
  864.1 20.3 copy-start.65
  864.1 20.3 copy-start.67
  864.1 20.3 copy-start.69
  912.0 419.1 %reduce-scatter.24.cloned.1.call-start = ((), (), s32[]{:S(2)}) async-start(), calls=%async_computation.13 | async-start | bytes 442368
  914.8 12.9 copy-start.21
  933.3 13.4 copy-start.60
  933.3 13.4 copy-start.61
  947.7 384.8 %reduce-scatter.26.cloned.1.call-start = ((), (), s32[]{:S(2)}) async-start(), calls=%async_computation.14 | async-start | bytes 1179648
  950.6 467.5 %reduce-scatter.22.cloned.1.call-start = ((), (), s32[]{:S(2)}) async-start(), calls=%async_computation.12 | async-start | bytes 1081344
  1215.5 763.8 %all-reduce.5.cloned.1.call-start = ((), (), s32[]{:S(2)}) async-start(), calls=%async_computation.15 | async-start | bytes 33554432 | tf_op jit(solution)/shard_map/psum | solution.py:164
  1224.8 808.4 %reduce-scatter.16.cloned.1.call-start = ((), (), s32[]{:S(2)}) async-start(), calls=%async_computation.9 | async-start | bytes 4718592 | tf_op jit(solution)/shard_map/reduce_scatter | solution.py:242
  1236.4 893.2 %reduce-scatter.14.cloned.1.call-start = ((), (), s32[]{:S(2)}) async-start(), calls=%async_computation.8 | async-start | bytes 14155776 | tf_op jit(solution)/shard_map/reduce_scatter | solution.py:241
  1242.7 9.6 copy-start.35
  1265.5 984.5 %reduce-scatter.18.cloned.1.call-start = ((), (), s32[]{:S(2)}) async-start(), calls=%async_computation.10 | async-start | bytes 18874368 | tf_op jit(solution)/shard_map/reduce_scatter | solution.py:243
  1265.7 15.6 copy-start.27
  1265.7 15.6 copy-start.91
  1297.3 1072.7 %reduce-scatter.20.cloned.1.call-start = ((), (), s32[]{:S(2)}) async-start(), calls=%async_computation.11 | async-start | bytes 18874368 | tf_op jit(solution)/shard_map/reduce_scatter | solution.py:244
  1297.5 15.5 copy-start.89
  1419.2 950.8 %copy-start.85 = (f32[1,64]{1,0:T(1,128)}, f32[1,64]{1,0:T(1,128)S(1)}, u32[]{:S(2)}) copy-start(f32[1,64]{1,0:T(1,128)S(1)} %copy.162) | copy-start | bytes 772
  (74 other events, 302.8 us)
Sparse Core Ops, SparseCore 0:
  66.8 293.5 all-gather.1
  912.1 291.8 all-reduce.6
  1207.0 32.8 reduce-scatter.23
  1243.0 35.9 reduce-scatter.25
  1281.1 137.0 reduce-scatter.21
  1420.6 558.5 all-reduce.4
  1983.2 49.9 reduce-scatter.15
  2037.3 92.3 reduce-scatter.13
  2133.8 116.1 reduce-scatter.17
  2254.0 115.9 reduce-scatter.19
